TPU v7x, 256 devices: a whole 4x4x8 slice. The times are simulated.
256 devices in a mesh: dp: 8 (over y, x_hi), expert: 8 (over z), tensor: 4 (over x_lo, core).
Axes of the slice: x: 4 (x_hi: 2, x_lo: 2; x = x_hi * 2 + x_lo), y: 4, z: 8, core: 2. Of those that a mesh axis runs over, the one named last changes fastest.
Arguments:
- tokens: bfloat16 [4096, 2048], P(('dp', 'expert', 'tensor')), may hold values from -6 to 6
- cotangent: bfloat16 [4096, 2048], P(('dp', 'expert', 'tensor')), may hold values from -3 to 3
- routes: int32 [4096, 2], P(('dp', 'expert', 'tensor')), may hold values from 0 to 7, all different within a row; in each aligned block of 16 rows (0 to 15, 16 to 31, ...) at most 5 rows name the same one
- weight_codes: int32 [4096, 2], P(('dp', 'expert', 'tensor')), may hold values from 16 to 256
- dense_gate: bfloat16 [2048, 8192], P('expert', ('dp', 'tensor')), may hold values from -0.125 to 0.125
- dense_up: bfloat16 [2048, 8192], P('expert', ('dp', 'tensor')), may hold values from -0.125 to 0.125
- dense_down_t: bfloat16 [2048, 8192], P('expert', ('dp', 'tensor')), may hold values from -0.0625 to 0.0625
Outputs:
- mixed: bfloat16 [4096, 2048], P(('dp', 'expert', 'tensor'))
- input_grad: bfloat16 [4096, 2048], P(('dp', 'expert', 'tensor'))
- grad_gate: bfloat16 [8, 2048, 8192], P('expert', None, ('dp', 'tensor'))
- grad_up: bfloat16 [8, 2048, 8192], P('expert', None, ('dp', 'tensor'))
- grad_down_t: bfloat16 [8, 2048, 8192], P('expert', None, ('dp', 'tensor'))
Inputs may be any that keep to these rules, and one draw needn't show every extreme that they name: `routes`: each row names two different experts; the rows of one device name each expert at most 5 times.
All inputs are finite; a program needn't handle non-finite values.
Results may differ from a plain program's by a relative error of at most 0.02.
Values may be sent and summed in bfloat16 or wider, within the bound.
No kernel may reach another device: no remote copies, remote signals or barrier semaphores. Data moves between devices by JAX's collectives and lax.ppermute only.
A program may use at most 128 MiB of HBM per device.

v0:
```python
import jax
import jax.numpy as jnp
from jax import lax
from jax.sharding import PartitionSpec as P


def silu_parts(gate_pre):
    sigmoid_val = jax.nn.sigmoid(gate_pre)
    return (gate_pre * sigmoid_val, sigmoid_val * (1.0 + gate_pre * (1.0 - sigmoid_val)))


def contract_rows(left_side, right_side):
    return lax.dot_general(
        left_side, right_side, (((0,), (0,)), ((), ())), preferred_element_type=jnp.float32
    )


def contract_cols(left_side, right_side):
    return lax.dot_general(
        left_side, right_side, (((1,), (1,)), ((), ())), preferred_element_type=jnp.float32
    )


def expert_rows(rows_x, rows_dy, rows_code, gate_cols, up_cols, down_cols):
    gate_pre = jnp.dot(rows_x, gate_cols, preferred_element_type=jnp.float32)
    up_pre = jnp.dot(rows_x, up_cols, preferred_element_type=jnp.float32)
    activation, act_slope = silu_parts(gate_pre)
    hidden = (activation * up_pre).astype(jnp.bfloat16)
    code_scale = rows_code.astype(jnp.float32) / 256.0
    scaled = (code_scale[:, None] * rows_dy.astype(jnp.float32)).astype(jnp.bfloat16)
    hidden_grad = jnp.dot(scaled, down_cols, preferred_element_type=jnp.float32)
    gate_grad = (hidden_grad * up_pre * act_slope).astype(jnp.bfloat16)
    up_grad = (hidden_grad * activation).astype(jnp.bfloat16)
    weight_grads = (
        contract_rows(rows_x, gate_grad),
        contract_rows(rows_x, up_grad),
        contract_rows(scaled, hidden),
    )
    return (hidden, gate_grad, up_grad, weight_grads)


def shards(tokens, cotangent, routes, weight_codes, dense_gate, dense_up, dense_down_t):
    gate_cols, up_cols, down_cols = (
        lax.all_gather(dense_gate, "expert", axis=0, tiled=True),
        lax.all_gather(dense_up, "expert", axis=0, tiled=True),
        lax.all_gather(dense_down_t, "expert", axis=0, tiled=True),
    )
    experts = lax.axis_size("expert")
    count_tok, model_width = tokens.shape
    capacity = 5 * count_tok // (2 * experts)
    slots_here = experts * capacity
    flat_route = routes.reshape(-1)
    flat_code = weight_codes.reshape(-1)
    onehot = (flat_route[:, None] == jnp.arange(experts, dtype=jnp.int32)[None, :]).astype(
        jnp.int32
    )
    earlier = jnp.cumsum(onehot, axis=0) - onehot
    slot_of = flat_route * capacity + jnp.sum(earlier * onehot, axis=1)
    placed = (slot_of[None, :] == jnp.arange(slots_here, dtype=jnp.int32)[:, None]).astype(
        jnp.int32
    )
    placed_tok = placed.reshape(slots_here, count_tok, 2).sum(axis=2)
    place_table = placed_tok.astype(jnp.bfloat16)
    send_x = jnp.dot(place_table, tokens, preferred_element_type=jnp.float32).astype(jnp.bfloat16)
    send_dy = jnp.dot(place_table, cotangent, preferred_element_type=jnp.float32).astype(
        jnp.bfloat16
    )
    send_code = jnp.sum(placed * flat_code[None, :], axis=1)
    parcel = (
        lax.all_to_all(
            send_x.reshape(experts, capacity, model_width),
            "expert",
            split_axis=0,
            concat_axis=0,
            tiled=True,
        ),
        lax.all_to_all(
            send_dy.reshape(experts, capacity, model_width),
            "expert",
            split_axis=0,
            concat_axis=0,
            tiled=True,
        ),
        lax.all_to_all(
            send_code.reshape(experts, capacity), "expert", split_axis=0, concat_axis=0, tiled=True
        ),
    )
    parcel = (
        lax.all_gather(parcel[0], ("dp", "tensor"), axis=0, tiled=True),
        lax.all_gather(parcel[1], ("dp", "tensor"), axis=0, tiled=True),
        lax.all_gather(parcel[2], ("dp", "tensor"), axis=0, tiled=True),
    )
    all_x = parcel[0].reshape(-1, model_width)
    all_dy = parcel[1].reshape(-1, model_width)
    all_code = parcel[2].reshape(-1)
    hidden, gate_grad, up_grad, weight_grads = expert_rows(
        all_x, all_dy, all_code, gate_cols, up_cols, down_cols
    )
    out_rows = lax.psum_scatter(
        contract_cols(hidden, down_cols).astype(jnp.bfloat16),
        ("dp", "tensor"),
        scatter_dimension=0,
        tiled=True,
    )
    grad_rows = lax.psum_scatter(
        (contract_cols(gate_grad, gate_cols) + contract_cols(up_grad, up_cols)).astype(
            jnp.bfloat16
        ),
        ("dp", "tensor"),
        scatter_dimension=0,
        tiled=True,
    )
    back_out, back_grad = (
        lax.all_to_all(
            out_rows.reshape(experts, capacity, model_width),
            "expert",
            split_axis=0,
            concat_axis=0,
            tiled=True,
        ),
        lax.all_to_all(
            grad_rows.reshape(experts, capacity, model_width),
            "expert",
            split_axis=0,
            concat_axis=0,
            tiled=True,
        ),
    )
    code_scale = flat_code.astype(jnp.float32) / 256.0
    weighted = (
        (placed.astype(jnp.float32) * code_scale[None, :])
        .reshape(slots_here, count_tok, 2)
        .sum(axis=2)
    )
    mixed = lax.dot_general(
        weighted,
        back_out.reshape(slots_here, model_width).astype(jnp.float32),
        (((0,), (0,)), ((), ())),
        precision=lax.Precision.HIGHEST,
        preferred_element_type=jnp.float32,
    ).astype(jnp.bfloat16)
    input_grad = contract_rows(place_table, back_grad.reshape(slots_here, model_width)).astype(
        jnp.bfloat16
    )
    grad_gate = weight_grads[0].astype(jnp.bfloat16)[None]
    grad_up = weight_grads[1].astype(jnp.bfloat16)[None]
    grad_down_t = weight_grads[2].astype(jnp.bfloat16)[None]
    return (mixed, input_grad, grad_gate, grad_up, grad_down_t)


def solution(mesh):
    placed = (
        P(("dp", "expert", "tensor"), None),
        P(("dp", "expert", "tensor"), None),
        P(("dp", "expert", "tensor"), None),
        P(("dp", "expert", "tensor"), None),
        P("expert", ("dp", "tensor")),
        P("expert", ("dp", "tensor")),
        P("expert", ("dp", "tensor")),
    )
    return jax.shard_map(
        shards,
        mesh=mesh,
        in_specs=placed,
        out_specs=(
            P(("dp", "expert", "tensor"), None),
            P(("dp", "expert", "tensor"), None),
            P("expert", None, ("dp", "tensor")),
            P("expert", None, ("dp", "tensor")),
            P("expert", None, ("dp", "tensor")),
        ),
        check_vma=False,
    )
```

profile of v0, /device:TPU:2, one launch (start us, length us, event | category | flops | bytes accessed | tf_op | source)
XLA Modules:
  0.0 478.8 jit_solution(12512945700379093156)
XLA Ops:
  9.6 20.1 %all_to_all.32 = bf16[8,5,2048]{2,1,0:T(8,128)(2,1)S(1)} all-to-all(bf16[8,5,2048]{2,1,0:T(8,128)(2,1)S(1)} %reshape.89), channel_id=1, replica_groups=mesh['dp'=8,'expert'=8,'tensor'=4] {'expert'}, dimensions={0} | all-to-all | bytes 327680 | tf_op jit(solution)/shard_map/all_to_all | solution.py:70
  31.8 12.9 %all_to_all.33 = bf16[8,5,2048]{2,1,0:T(8,128)(2,1)S(1)} all-to-all(bf16[8,5,2048]{2,1,0:T(8,128)(2,1)S(1)} %reshape.93), channel_id=1, replica_groups=mesh['dp'=8,'expert'=8,'tensor'=4] {'expert'}, dimensions={0} | all-to-all | bytes 327680 | tf_op jit(solution)/shard_map/all_to_all | solution.py:77
  48.5 10.0 %all_to_all.34 = s32[8,1,5]{2,1,0:T(1,128)S(1)} all-to-all(s32[8,1,5]{2,1,0:T(1,128)S(1)} %bitcast.28), channel_id=1, replica_groups=mesh['dp'=8,'expert'=8,'tensor'=4] {'expert'}, dimensions={0} | all-to-all | bytes 320 | tf_op jit(solution)/shard_map/all_to_all | solution.py:84
  58.5 24.6 %all-gather = s32[256,1,5]{2,1,0:T(1,128)S(1)} all-gather(s32[8,1,5]{2,1,0:T(1,128)S(1)} %all_to_all.34), channel_id=2, replica_groups=mesh['dp'=8,'expert'=8,'tensor'=4] {'dp','tensor'}, dimensions={0}, use_global_device_ids=true | all-gather | bytes 5280 | tf_op jit(solution)/shard_map/all_gather | solution.py:91
  83.7 8.9 %copy.55 = bf16[256,5,2048]{2,1,0:T(8,128)(2,1)} copy(bf16[256,5,2048]{2,0,1:T(8,128)(2,1)} %all-gather.7.cloned.1.call-done) | data formatting | bytes 10485760 | tf_op jit(solution)/shard_map/all_gather | solution.py:89
  92.7 10.0 %reshape.90 = bf16[1280,2048]{1,0:T(8,128)(2,1)} reshape(bf16[256,5,2048]{2,1,0:T(8,128)(2,1)} %copy.55) | data formatting | bytes 10485760 | tf_op jit(solution)/shard_map/reshape | solution.py:93
  102.7 31.9 %all-gather.15.cloned.1.call-done = bf16[256,5,2048]{2,0,1:T(8,128)(2,1)} async-done(((bf16[8,5,2048]{2,0,1:T(8,128)(2,1)}), bf16[256,5,2048]{2,0,1:T(8,128)(2,1)}) %all-gather.15.cloned.1.call-update) | async-done | bytes 5242896 | tf_op jit(solution)/shard_map/all_gather | solution.py:90
  134.6 11.5 %copy.59 = f32[256,5,2048]{2,1,0:T(8,128)} copy(bf16[256,5,2048]{2,0,1:T(8,128)(2,1)} %all-gather.15.cloned.1.call-done) | data formatting | bytes 15728640 | tf_op jit(solution)/shard_map/convert_element_type | solution.py:30
  146.1 14.1 %reshape.96 = f32[1280,2048]{1,0:T(8,128)} reshape(f32[256,5,2048]{2,1,0:T(8,128)} %copy.59) | data formatting | bytes 20971520 | tf_op jit(solution)/shard_map/convert_element_type | solution.py:30
  160.2 14.7 %all-gather.9.cloned.1.call-done = bf16[2048,256]{1,0:T(8,128)(2,1)} async-done(((bf16[256,256]{1,0:T(8,128)(2,1)}), bf16[2048,256]{1,0:T(8,128)(2,1)}) %all-gather.9.cloned.1.call-update) | async-done | bytes 1048592 | tf_op jit(solution)/shard_map/all_gather | solution.py:44
  174.9 5.4 %fusion.11 = f32[1280,256]{1,0:T(8,128)} fusion(bf16[1280,2048]{1,0:T(8,128)(2,1)} %reshape.90, bf16[2048,256]{1,0:T(8,128)(2,1)} %all-gather.9.cloned.1.call-done), kind=kOutput, calls=%fused_computation.36 | convolution fusion | flops 1342177280 | bytes 7602176 | tf_op jit(solution)/shard_map/dot_general | solution.py:25
  180.3 33.5 %all-gather.11.cloned.1.call-done = bf16[2048,256]{1,0:T(8,128)(2,1)} async-done(((bf16[256,256]{1,0:T(8,128)(2,1)}), bf16[2048,256]{1,0:T(8,128)(2,1)}) %all-gather.11.cloned.1.call-update) | async-done | bytes 1048592 | tf_op jit(solution)/shard_map/all_gather | solution.py:45
  213.8 5.4 %fusion.12 = f32[1280,256]{1,0:T(8,128)} fusion(bf16[1280,2048]{1,0:T(8,128)(2,1)} %reshape.90, bf16[2048,256]{1,0:T(8,128)(2,1)} %all-gather.11.cloned.1.call-done), kind=kOutput, calls=%fused_computation.37 | convolution fusion | flops 1342177280 | bytes 7602176 | tf_op jit(solution)/shard_map/dot_general | solution.py:26
  219.1 33.5 %all-gather.13.cloned.1.call-done = bf16[2048,256]{1,0:T(8,128)(2,1)} async-done(((bf16[256,256]{1,0:T(8,128)(2,1)}), bf16[2048,256]{1,0:T(8,128)(2,1)}) %all-gather.13.cloned.1.call-update) | async-done | bytes 1048592 | tf_op jit(solution)/shard_map/all_gather | solution.py:46
  252.6 7.0 %multiply_convert_fusion.1 = (bf16[1280,256]{1,0:T(8,128)(2,1)S(1)}, bf16[1280,256]{1,0:T(8,128)(2,1)S(1)}, bf16[1280,256]{1,0:T(8,128)(2,1)S(1)}) fusion(f32[1280,256]{1,0:T(8,128)} %fusion.11, f32[1280,256]{1,0:T(8,128)} %fusion.12, bf16[2048,256]{1,0:T(8,128)(2,1)} %all-gather.13.cloned.1.call-done, f32[1280,2048]{1,0:T(8,128)} %reshape.96, ...), kind=kOutput, calls=%fused_computation.13 | convolution fusion | flops 1352335360 | bytes 16126976 | tf_op jit(solution)/shard_map/dot_general | solution.py:31
  266.4 3.9 convolution_convert_fusion
  271.0 6.9 %fusion.2 = bf16[1,2048,256]{2,1,0:T(8,128)(2,1)} fusion(bf16[1280,256]{1,0:T(8,128)(2,1)S(1)} %get-tuple-element.7, f32[1280,2048]{1,0:T(8,128)} %reshape.96, f32[1280]{0:T(1024)S(1)} %div.22), kind=kOutput, calls=%fused_computation.8 | convolution fusion | flops 1347944448 | bytes 12194816 | tf_op jit(solution)/shard_map/dot_general | solution.py:13
  277.9 77.7 %reduce-scatter.5.cloned.1.call-done = bf16[40,2048]{1,0:T(8,128)(2,1)} async-done(((bf16[1280,2048]{1,0:T(8,128)(2,1)}), bf16[40,2048]{1,0:T(8,128)(2,1)}) %reduce-scatter.5.cloned.1.call-update) | async-done | bytes 163856 | tf_op jit(solution)/shard_map/reduce_scatter | solution.py:105
  357.4 7.0 %all-to-all-start.4 = ((bf16[8,5,2048]{2,1,0:T(8,128)(2,1)}), bf16[8,5,2048]{2,1,0:T(8,128)(2,1)S(1)}, u32[]{:S(2)}, u32[]{:S(2)}) async-start(bf16[8,5,2048]{2,1,0:T(8,128)(2,1)} %reshape.94), calls=%async_computation.6 | async-start | bytes 524288 | tf_op jit(solution)/shard_map/all_to_all | solution.py:121
  364.4 5.1 %fusion = bf16[1,2048,256]{2,1,0:T(8,128)(2,1)} fusion(bf16[1280,2048]{1,0:T(8,128)(2,1)} %reshape.90, bf16[1280,256]{1,0:T(8,128)(2,1)S(1)} %get-tuple-element.6), kind=kOutput, calls=%fused_computation.6 | convolution fusion | flops 1342701568 | bytes 6946816 | tf_op jit(solution)/shard_map/dot_general | solution.py:13
  369.5 82.4 %reduce-scatter.3.cloned.1.call-done = bf16[40,2048]{1,0:T(8,128)(2,1)} async-done(((bf16[1280,2048]{1,0:T(8,128)(2,1)}), bf16[40,2048]{1,0:T(8,128)(2,1)}) %reduce-scatter.3.cloned.1.call-update) | async-done | bytes 163856 | tf_op jit(solution)/shard_map/reduce_scatter | solution.py:99
  453.5 7.0 %all-to-all-start.1 = ((bf16[8,5,2048]{2,1,0:T(8,128)(2,1)}), bf16[8,5,2048]{2,1,0:T(8,128)(2,1)S(1)}, u32[]{:S(2)}, u32[]{:S(2)}) async-start(bf16[8,5,2048]{2,1,0:T(8,128)(2,1)} %reshape.91), calls=%async_computation.2 | async-start | bytes 524288 | tf_op jit(solution)/shard_map/all_to_all | solution.py:114
  460.5 5.1 %fusion.1 = bf16[1,2048,256]{2,1,0:T(8,128)(2,1)} fusion(bf16[1280,2048]{1,0:T(8,128)(2,1)} %reshape.90, bf16[1280,256]{1,0:T(8,128)(2,1)S(1)} %get-tuple-element.5), kind=kOutput, calls=%fused_computation.7 | convolution fusion | flops 1342701568 | bytes 6946816 | tf_op jit(solution)/shard_map/dot_general | solution.py:13
  466.5 4.5 all-to-all-done.1
  (60 shorter events, 21.3 us)
Async XLA Ops:
  7.2 2.2 copy-start
  7.2 76.6 %all-gather.7.cloned.1.call-start = ((), (), s32[]{:S(2)}) async-start(), calls=%async_computation.7 | async-start | bytes 5406720 | tf_op jit(solution)/shard_map/all_gather | solution.py:89
  30.6 104.0 %all-gather.15.cloned.1.call-start = ((), (), s32[]{:S(2)}) async-start(), calls=%async_computation.12 | async-start | bytes 5406720 | tf_op jit(solution)/shard_map/all_gather | solution.py:90
  45.5 129.4 %all-gather.9.cloned.1.call-start = ((), (), s32[]{:S(2)}) async-start(), calls=%async_computation.8 | async-start | bytes 1179648 | tf_op jit(solution)/shard_map/all_gather | solution.py:44
  46.3 167.5 %all-gather.11.cloned.1.call-start = ((), (), s32[]{:S(2)}) async-start(), calls=%async_computation.9 | async-start | bytes 1179648 | tf_op jit(solution)/shard_map/all_gather | solution.py:45
  46.8 205.8 %all-gather.13.cloned.1.call-start = ((), (), s32[]{:S(2)}) async-start(), calls=%async_computation.10 | async-start | bytes 1179648 | tf_op jit(solution)/shard_map/all_gather | solution.py:46
  47.4 308.3 %reduce-scatter.5.cloned.1.call-start = ((), (), s32[]{:S(2)}) async-start(), calls=%async_computation.13 | async-start | bytes 5406720 | tf_op jit(solution)/shard_map/reduce_scatter | solution.py:105
  219.1 40.6 %copy-start.2 = (bf16[2048,256]{1,0:T(8,128)(2,1)S(1)}, bf16[2048,256]{1,0:T(8,128)(2,1)}, u32[]{:S(2)}) copy-start(bf16[2048,256]{1,0:T(8,128)(2,1)} %all-gather.9.cloned.1.call-done) | copy-start | bytes 3145732
  259.7 1.6 copy-start.4
  265.1 1.2 copy-start.3
  265.2 186.7 %reduce-scatter.3.cloned.1.call-start = ((), (), s32[]{:S(2)}) async-start(), calls=%async_computation.11 | async-start | bytes 5406720 | tf_op jit(solution)/shard_map/reduce_scatter | solution.py:99
  270.3 0.7 copy-start.5
  357.4 96.1 %all-to-all-start.4 = ((bf16[8,5,2048]{2,1,0:T(8,128)(2,1)}), bf16[8,5,2048]{2,1,0:T(8,128)(2,1)S(1)}, u32[]{:S(2)}, u32[]{:S(2)}) async-start(bf16[8,5,2048]{2,1,0:T(8,128)(2,1)} %reshape.94), calls=%async_computation.6 | async-start | bytes 524288 | tf_op jit(solution)/shard_map/all_to_all | solution.py:121
  453.5 17.5 %all-to-all-start.1 = ((bf16[8,5,2048]{2,1,0:T(8,128)(2,1)}), bf16[8,5,2048]{2,1,0:T(8,128)(2,1)S(1)}, u32[]{:S(2)}, u32[]{:S(2)}) async-start(bf16[8,5,2048]{2,1,0:T(8,128)(2,1)} %reshape.91), calls=%async_computation.2 | async-start | bytes 524288 | tf_op jit(solution)/shard_map/all_to_all | solution.py:114
  460.5 11.4 %copy-start.1 = (bf16[16,2048]{1,0:T(8,128)(2,1)S(1)}, bf16[16,2048]{1,0:T(8,128)(2,1)}, u32[]{:S(2)}) copy-start(bf16[16,2048]{1,0:T(8,128)(2,1)} %param.7) | copy-start | bytes 196612
Sparse Core Ops, SparseCore 0:
  30.7 48.5 all-gather.6
  82.5 52.0 all-gather.14
  136.4 38.4 all-gather.8
  176.5 37.1 all-gather.10
  215.4 37.1 all-gather.12
  265.3 90.3 reduce-scatter.4
  360.2 91.5 reduce-scatter.2
where the time goes:
time: 480 us; the launch traced here: 479 us
  waiting for transfers between devices  280 us (58%)
  blocking collectives  67.7 us (14%)
  local copies, waits for them, and re-layouts  53.5 us (11%)
  matrix products  47.1 us (10%)
  starting transfers between devices  14.6 us (3%)
  between operations  14.3 us (3%)
    reduce_scatter x1, waiting for transfers between devices, shards(): lax.psum_scatter(contract_cols(hidden, down_cols).astype(jnp.bfloat16), (...  82.4 us
    reduce_scatter x1, waiting for transfers between devices, shards(): lax.psum_scatter((contract_cols(gate_grad, gate_cols) + contract_cols(up_...  77.7 us
    all_gather x1, waiting for transfers between devices, shards(): lax.all_gather(dense_down_t, 'expert', axis=0, tiled=True)  33.5 us
    all_gather x1, waiting for transfers between devices, shards(): lax.all_gather(dense_up, 'expert', axis=0, tiled=True)  33.5 us
    all_gather x1, waiting for transfers between devices, shards(): lax.all_gather(parcel[1], ('dp', 'tensor'), axis=0, tiled=True)  31.9 us
    convert_element_type x2, local copies, waits for them, and re-layouts, expert_rows(): rows_dy.astype(jnp.float32)  25.6 us
    all_gather x1, blocking collectives, shards(): lax.all_gather(parcel[2], ('dp', 'tensor'), axis=0, tiled=True)  24.6 us
    all_to_all x1, blocking collectives, shards(): lax.all_to_all(send_x.reshape(experts, capacity, model_width), 'expert',...  20.1 us
  transfers between devices with their start and end apart: 9, of which 7 were waited for; matrix products, arithmetic and copies ran while one was open for 18% of the time, Pallas kernels for 0%

commit v1 on v0

--- a/solution.py
+++ b/solution.py
@@ -41,7 +41,10 @@
 
 def shards(tokens, cotangent, routes, weight_codes, dense_gate, dense_up, dense_down_t):
     gate_cols, up_cols, down_cols = (
-        lax.all_gather(dense_gate, "expert", axis=0, tiled=True),
+        jnp.concatenate(
+            lax.all_to_all(jnp.stack([dense_gate] * lax.axis_size("expert")), "expert", 0, 0),
+            axis=0,
+        ),
         lax.all_gather(dense_up, "expert", axis=0, tiled=True),
         lax.all_gather(dense_down_t, "expert", axis=0, tiled=True),
     )

time: 480 us -> 441 us (0.919)
  waiting for transfers between devices: 280 us -> 236 us
    all_gather x1, waiting for transfers between devices: 33.5 us -> 9.62 us  [shards(): lax.all_gather(dense_up, 'expert', axis=0, tiled=True)]
    all_gather x1 -> x0, waiting for transfers between devices: 14.7 us -> none  [shards(): lax.all_gather(dense_gate, 'expert', axis=0, tiled=True)]
    all_gather x1, waiting for transfers between devices: 31.9 us -> 26.9 us  [shards(): lax.all_gather(parcel[1], ('dp', 'tensor'), axis=0, tiled=True)]
  transfers between devices with their start and end apart: 9 -> 9, of which waited for: 7 -> 6; matrix products, arithmetic and copies ran while one was open for 18% -> 19% of each run, Pallas kernels for 0% -> 0%
where the time goes in v1:
time: 441 us; the launch traced here: 440 us
  waiting for transfers between devices  236 us (54%)
  blocking collectives  67.7 us (15%)
  local copies, waits for them, and re-layouts  55.4 us (13%)
  matrix products  46.8 us (11%)
  starting transfers between devices  18.1 us (4%)
  between operations  14.2 us (3%)
    reduce_scatter x1, waiting for transfers between devices, shards(): lax.psum_scatter(contract_cols(hidden, down_cols).astype(jnp.bfloat16), (...  82.3 us
    reduce_scatter x1, waiting for transfers between devices, shards(): lax.psum_scatter((contract_cols(gate_grad, gate_cols) + contract_cols(up_...  77.7 us
    all_gather x1, waiting for transfers between devices, shards(): lax.all_gather(dense_down_t, 'expert', axis=0, tiled=True)  33.5 us
    all_gather x1, waiting for transfers between devices, shards(): lax.all_gather(parcel[1], ('dp', 'tensor'), axis=0, tiled=True)  26.9 us
    convert_element_type x2, local copies, waits for them, and re-layouts, expert_rows(): rows_dy.astype(jnp.float32)  25.6 us
    all_gather x1, blocking collectives, shards(): lax.all_gather(parcel[2], ('dp', 'tensor'), axis=0, tiled=True)  24.6 us
    all_to_all x1, blocking collectives, shards(): lax.all_to_all(send_x.reshape(experts, capacity, model_width), 'expert',...  20.1 us
    dot_general x4, matrix products, contract_rows(): lax.dot_general(left_side, right_side, (((0,), (0,)), ((), ())), preferre...  17.9 us
  transfers between devices with their start and end apart: 9, of which 6 were waited for; matrix products, arithmetic and copies ran while one was open for 19% of the time, Pallas kernels for 0%

profile of v1, /device:TPU:2, one launch (start us, length us, event | category | flops | bytes accessed | tf_op | source)
XLA Modules:
  0.0 439.8 jit_solution(5025979527332592818)
XLA Ops:
  9.6 20.1 %all_to_all.37 = bf16[8,5,2048]{2,1,0:T(8,128)(2,1)S(1)} all-to-all(bf16[8,5,2048]{2,1,0:T(8,128)(2,1)S(1)} %reshape.94), channel_id=1, replica_groups=mesh['dp'=8,'expert'=8,'tensor'=4] {'expert'}, dimensions={0} | all-to-all | bytes 327680 | tf_op jit(solution)/shard_map/all_to_all | solution.py:73
  31.8 12.9 %all_to_all.38 = bf16[8,5,2048]{2,1,0:T(8,128)(2,1)S(1)} all-to-all(bf16[8,5,2048]{2,1,0:T(8,128)(2,1)S(1)} %reshape.99), channel_id=1, replica_groups=mesh['dp'=8,'expert'=8,'tensor'=4] {'expert'}, dimensions={0} | all-to-all | bytes 327680 | tf_op jit(solution)/shard_map/all_to_all | solution.py:80
  47.3 10.0 %all_to_all.39 = s32[8,1,5]{2,1,0:T(1,128)S(1)} all-to-all(s32[8,1,5]{2,1,0:T(1,128)S(1)} %bitcast.31), channel_id=1, replica_groups=mesh['dp'=8,'expert'=8,'tensor'=4] {'expert'}, dimensions={0} | all-to-all | bytes 320 | tf_op jit(solution)/shard_map/all_to_all | solution.py:87
  63.5 24.6 %all-gather = s32[256,1,5]{2,1,0:T(1,128)S(1)} all-gather(s32[8,1,5]{2,1,0:T(1,128)S(1)} %all_to_all.39), channel_id=2, replica_groups=mesh['dp'=8,'expert'=8,'tensor'=4] {'dp','tensor'}, dimensions={0}, use_global_device_ids=true | all-gather | bytes 5280 | tf_op jit(solution)/shard_map/all_gather | solution.py:94
  88.7 8.9 %copy.55 = bf16[256,5,2048]{2,1,0:T(8,128)(2,1)} copy(bf16[256,5,2048]{2,0,1:T(8,128)(2,1)} %all-gather.6.cloned.1.call-done) | data formatting | bytes 10485760 | tf_op jit(solution)/shard_map/all_gather | solution.py:92
  97.6 10.0 %reshape.95 = bf16[1280,2048]{1,0:T(8,128)(2,1)} reshape(bf16[256,5,2048]{2,1,0:T(8,128)(2,1)} %copy.55) | data formatting | bytes 10485760 | tf_op jit(solution)/shard_map/reshape | solution.py:96
  107.6 26.9 %all-gather.12.cloned.1.call-done = bf16[256,5,2048]{2,0,1:T(8,128)(2,1)} async-done(((bf16[8,5,2048]{2,0,1:T(8,128)(2,1)}), bf16[256,5,2048]{2,0,1:T(8,128)(2,1)}) %all-gather.12.cloned.1.call-update) | async-done | bytes 5242896 | tf_op jit(solution)/shard_map/all_gather | solution.py:93
  134.6 11.5 %copy.59 = f32[256,5,2048]{2,1,0:T(8,128)} copy(bf16[256,5,2048]{2,0,1:T(8,128)(2,1)} %all-gather.12.cloned.1.call-done) | data formatting | bytes 15728640 | tf_op jit(solution)/shard_map/convert_element_type | solution.py:30
  146.0 14.1 %reshape.102 = f32[1280,2048]{1,0:T(8,128)} reshape(f32[256,5,2048]{2,1,0:T(8,128)} %copy.59) | data formatting | bytes 20971520 | tf_op jit(solution)/shard_map/convert_element_type | solution.py:30
  160.1 5.1 %fusion.11 = f32[1280,256]{1,0:T(8,128)} fusion(bf16[1280,2048]{1,0:T(8,128)(2,1)} %reshape.95, bf16[2048,256]{1,0:T(8,128)(2,1)S(1)} %bitcast.29), kind=kOutput, calls=%fused_computation.36 | convolution fusion | flops 1342177280 | bytes 7602176 | tf_op jit(solution)/shard_map/dot_general | solution.py:25
  165.2 9.6 %all-gather.8.cloned.1.call-done = bf16[2048,256]{1,0:T(8,128)(2,1)} async-done(((bf16[256,256]{1,0:T(8,128)(2,1)}), bf16[2048,256]{1,0:T(8,128)(2,1)}) %all-gather.8.cloned.1.call-update) | async-done | bytes 1048592 | tf_op jit(solution)/shard_map/all_gather | solution.py:48
  174.9 5.4 %fusion.12 = f32[1280,256]{1,0:T(8,128)} fusion(bf16[1280,2048]{1,0:T(8,128)(2,1)} %reshape.95, bf16[2048,256]{1,0:T(8,128)(2,1)} %all-gather.8.cloned.1.call-done), kind=kOutput, calls=%fused_computation.37 | convolution fusion | flops 1342177280 | bytes 7602176 | tf_op jit(solution)/shard_map/dot_general | solution.py:26
  180.2 33.5 %all-gather.10.cloned.1.call-done = bf16[2048,256]{1,0:T(8,128)(2,1)} async-done(((bf16[256,256]{1,0:T(8,128)(2,1)}), bf16[2048,256]{1,0:T(8,128)(2,1)}) %all-gather.10.cloned.1.call-update) | async-done | bytes 1048592 | tf_op jit(solution)/shard_map/all_gather | solution.py:49
  213.7 7.0 %multiply_convert_fusion.1 = (bf16[1280,256]{1,0:T(8,128)(2,1)S(1)}, bf16[1280,256]{1,0:T(8,128)(2,1)S(1)}, bf16[1280,256]{1,0:T(8,128)(2,1)S(1)}) fusion(f32[1280,256]{1,0:T(8,128)} %fusion.11, f32[1280,256]{1,0:T(8,128)} %fusion.12, bf16[2048,256]{1,0:T(8,128)(2,1)} %all-gather.10.cloned.1.call-done, f32[1280,2048]{1,0:T(8,128)} %reshape.102, ...), kind=kOutput, calls=%fused_computation.13 | convolution fusion | flops 1352335360 | bytes 16126976 | tf_op jit(solution)/shard_map/dot_general | solution.py:31
  222.4 3.9 add_convert_fusion
  227.5 3.9 convolution_convert_fusion
  232.1 6.9 %fusion.2 = bf16[1,2048,256]{2,1,0:T(8,128)(2,1)} fusion(bf16[1280,256]{1,0:T(8,128)(2,1)S(1)} %get-tuple-element.7, f32[1280,2048]{1,0:T(8,128)} %reshape.102, f32[1280]{0:T(1024)S(1)} %div.22), kind=kOutput, calls=%fused_computation.8 | convolution fusion | flops 1347944448 | bytes 12194816 | tf_op jit(solution)/shard_map/dot_general | solution.py:13
  239.1 77.7 %reduce-scatter.5.cloned.1.call-done = bf16[40,2048]{1,0:T(8,128)(2,1)} async-done(((bf16[1280,2048]{1,0:T(8,128)(2,1)}), bf16[40,2048]{1,0:T(8,128)(2,1)}) %reduce-scatter.5.cloned.1.call-update) | async-done | bytes 163856 | tf_op jit(solution)/shard_map/reduce_scatter | solution.py:108
  318.4 7.0 %all-to-all-start.5 = ((bf16[8,5,2048]{2,1,0:T(8,128)(2,1)}), bf16[8,5,2048]{2,1,0:T(8,128)(2,1)S(1)}, u32[]{:S(2)}, u32[]{:S(2)}) async-start(bf16[8,5,2048]{2,1,0:T(8,128)(2,1)} %reshape.100), calls=%async_computation.7 | async-start | bytes 524288 | tf_op jit(solution)/shard_map/all_to_all | solution.py:124
  325.5 5.1 %fusion = bf16[1,2048,256]{2,1,0:T(8,128)(2,1)} fusion(bf16[1280,2048]{1,0:T(8,128)(2,1)} %reshape.95, bf16[1280,256]{1,0:T(8,128)(2,1)S(1)} %get-tuple-element.6), kind=kOutput, calls=%fused_computation.6 | convolution fusion | flops 1342701568 | bytes 6946816 | tf_op jit(solution)/shard_map/dot_general | solution.py:13
  330.5 82.3 %reduce-scatter.3.cloned.1.call-done = bf16[40,2048]{1,0:T(8,128)(2,1)} async-done(((bf16[1280,2048]{1,0:T(8,128)(2,1)}), bf16[40,2048]{1,0:T(8,128)(2,1)}) %reduce-scatter.3.cloned.1.call-update) | async-done | bytes 163856 | tf_op jit(solution)/shard_map/reduce_scatter | solution.py:102
  414.5 7.0 %all-to-all-start.2 = ((bf16[8,5,2048]{2,1,0:T(8,128)(2,1)}), bf16[8,5,2048]{2,1,0:T(8,128)(2,1)S(1)}, u32[]{:S(2)}, u32[]{:S(2)}) async-start(bf16[8,5,2048]{2,1,0:T(8,128)(2,1)} %reshape.97), calls=%async_computation.3 | async-start | bytes 524288 | tf_op jit(solution)/shard_map/all_to_all | solution.py:117
  421.5 5.1 %fusion.1 = bf16[1,2048,256]{2,1,0:T(8,128)(2,1)} fusion(bf16[1280,2048]{1,0:T(8,128)(2,1)} %reshape.95, bf16[1280,256]{1,0:T(8,128)(2,1)S(1)} %get-tuple-element.5), kind=kOutput, calls=%fused_computation.7 | convolution fusion | flops 1342701568 | bytes 6946816 | tf_op jit(solution)/shard_map/dot_general | solution.py:13
  427.5 4.5 %all-to-all-done.2 = bf16[8,5,2048]{2,1,0:T(8,128)(2,1)S(1)} async-done(((bf16[8,5,2048]{2,1,0:T(8,128)(2,1)}), bf16[8,5,2048]{2,1,0:T(8,128)(2,1)S(1)}, u32[]{:S(2)}, u32[]{:S(2)}) %all-to-all-start.2) | async-done | bytes 163872 | tf_op jit(solution)/shard_map/all_to_all | solution.py:117
  (58 shorter events, 22.3 us)
Async XLA Ops:
  7.2 2.2 copy-start
  7.2 81.5 %all-gather.6.cloned.1.call-start = ((), (), s32[]{:S(2)}) async-start(), calls=%async_computation.8 | async-start | bytes 5406720 | tf_op jit(solution)/shard_map/all_gather | solution.py:92
  30.6 104.0 %all-gather.12.cloned.1.call-start = ((), (), s32[]{:S(2)}) async-start(), calls=%async_computation.12 | async-start | bytes 5406720 | tf_op jit(solution)/shard_map/all_gather | solution.py:93
  45.5 129.3 %all-gather.8.cloned.1.call-start = ((), (), s32[]{:S(2)}) async-start(), calls=%async_computation.9 | async-start | bytes 1179648 | tf_op jit(solution)/shard_map/all_gather | solution.py:48
  59.3 100.9 %all-to-all-start.1 = ((bf16[8,256,256]{2,1,0:T(8,128)(2,1)}), bf16[8,256,256]{2,1,0:T(8,128)(2,1)S(1)}, u32[]{:S(2)}, u32[]{:S(2)}) async-start(bf16[8,256,256]{2,1,0:T(8,128)(2,1)} %stack.2), calls=%async_computation.1 | async-start | bytes 2097152 | tf_op jit(solution)/shard_map/all_to_all | solution.py:45
  62.8 150.9 %all-gather.10.cloned.1.call-start = ((), (), s32[]{:S(2)}) async-start(), calls=%async_computation.10 | async-start | bytes 1179648 | tf_op jit(solution)/shard_map/all_gather | solution.py:49
  63.4 253.3 %reduce-scatter.5.cloned.1.call-start = ((), (), s32[]{:S(2)}) async-start(), calls=%async_computation.13 | async-start | bytes 5406720 | tf_op jit(solution)/shard_map/reduce_scatter | solution.py:108
  220.8 1.6 copy-start.2
  226.3 1.2 copy-start.3
  226.3 186.5 %reduce-scatter.3.cloned.1.call-start = ((), (), s32[]{:S(2)}) async-start(), calls=%async_computation.11 | async-start | bytes 5406720 | tf_op jit(solution)/shard_map/reduce_scatter | solution.py:102
  231.4 0.7 copy-start.4
  318.4 96.1 %all-to-all-start.5 = ((bf16[8,5,2048]{2,1,0:T(8,128)(2,1)}), bf16[8,5,2048]{2,1,0:T(8,128)(2,1)S(1)}, u32[]{:S(2)}, u32[]{:S(2)}) async-start(bf16[8,5,2048]{2,1,0:T(8,128)(2,1)} %reshape.100), calls=%async_computation.7 | async-start | bytes 524288 | tf_op jit(solution)/shard_map/all_to_all | solution.py:124
  414.5 17.5 %all-to-all-start.2 = ((bf16[8,5,2048]{2,1,0:T(8,128)(2,1)}), bf16[8,5,2048]{2,1,0:T(8,128)(2,1)S(1)}, u32[]{:S(2)}, u32[]{:S(2)}) async-start(bf16[8,5,2048]{2,1,0:T(8,128)(2,1)} %reshape.97), calls=%async_computation.3 | async-start | bytes 524288 | tf_op jit(solution)/shard_map/all_to_all | solution.py:117
  421.5 11.4 %copy-start.1 = (bf16[16,2048]{1,0:T(8,128)(2,1)S(1)}, bf16[16,2048]{1,0:T(8,128)(2,1)}, u32[]{:S(2)}) copy-start(bf16[16,2048]{1,0:T(8,128)(2,1)} %param.7) | copy-start | bytes 196612
Sparse Core Ops, SparseCore 0:
  30.7 48.4 all-gather.5
  82.4 52.1 all-gather.11
  136.4 38.4 all-gather.7
  176.5 37.1 all-gather.9
  226.4 90.2 reduce-scatter.4
  321.1 91.6 reduce-scatter.2
